TPU v7x, 32 devices: a whole 2x2x4 slice. The times are simulated.
32 devices in a mesh: parts: 2 (over y), aux: 4 (over x, core), pair: 4 (over z).
Axes of the slice: x: 2, y: 2, z: 4, core: 2. Of those that a mesh axis runs over, the one named last changes fastest.
Arguments:
- cholesky: bfloat16 [96, 832, 832], P(('parts', 'aux', 'pair')), parts along dimension 0, may hold values from -1.5 to 1.5
- occ_coef: bfloat16 [2, 2, 832, 128], replicated, may hold values from -0.15625 to 0.15625
- vir_coef: bfloat16 [2, 2, 832, 1536], P(None, None, None, 'pair'), may hold values from -0.15625 to 0.15625
- occ_energy: float32 [128], replicated, may hold values from -3 to -0.3
- vir_energy: float32 [1536], replicated, may hold values from 0.2 to 3
- batch_occ: int32 [3], replicated, may hold values from 0 to 127, as said below
Outputs:
- pair_vectors: bfloat16 [96, 128, 2, 1536], P(('parts', 'aux', 'pair')), parts along dimension 0
- amplitudes: float32 [3072, 2, 3, 3, 1536], P(('parts', 'aux'), None, None, None, 'pair'), parts along dimension 0
There are 2 independent parts, one for each index of `parts`. A program takes and returns all parts, laid end to end along the dimension named above; an argument that names none is the same for every part. Nothing has to cross between parts.
Inputs may be any that keep to these rules, and one draw needn't show every extreme that they name: `batch_occ`: 3 distinct occupied indices, the highest occupied spinor 128 - 1 always among them.
All inputs are finite; a program needn't handle non-finite values.
Results may differ from a plain program's by a relative error of at most 0.0064.
Values may be sent and summed in bfloat16 or wider, within the bound.
No kernel may reach another device: no remote copies, remote signals or barrier semaphores. Data moves between devices by JAX's collectives and lax.ppermute only.
A program may use at most 192 MiB of HBM per device.

v0:
```python
import jax
import jax.numpy as jnp
from jax import lax
from jax.sharding import PartitionSpec as P


def complex_rows(half):
    real_part, imag_part = (half[..., :2, :], half[..., 2:, :])
    c0 = jnp.concatenate([real_part, -imag_part], -2)
    c1 = jnp.concatenate([imag_part, real_part], -2)
    return jnp.stack([c0, c1], -3)


def pair_terms(batch_rows, column_rows):
    left = jnp.concatenate([batch_rows[:, :, 0, :], batch_rows[:, :, 1, :]], 0)
    real_right = jnp.concatenate([column_rows[:, :, 0, :], -column_rows[:, :, 1, :]], 0)
    imag_right = jnp.concatenate([column_rows[:, :, 1, :], column_rows[:, :, 0, :]], 0)
    right = jnp.stack([real_right, imag_right], 1)
    return jnp.einsum("pjb,pcia->bcija", left, right, preferred_element_type=jnp.float32)


def on_device(cholesky, occ_coef, vir_coef, occ_energy, vir_energy, batch_occ):
    vectors = cholesky.shape[0]
    orbitals = cholesky.shape[1]
    occupied = occ_coef.shape[3]
    a_width = vir_coef.shape[3]
    n_pair = lax.axis_size("pair")
    n_aux = lax.axis_size("aux")
    n_parts = lax.axis_size("parts")
    rows = 4 * orbitals
    virtuals = n_pair * a_width
    occ_left = jnp.concatenate([occ_coef[0], -occ_coef[1]], 0)
    v_local = vir_coef.reshape(rows, a_width)
    occ_sel = jnp.take(occ_left, batch_occ, axis=2)
    half_sel = jnp.einsum(
        "kmi,pmn->pikn", occ_sel, cholesky, preferred_element_type=jnp.float32
    ).astype(jnp.bfloat16)
    half_sel_all = lax.all_gather(half_sel, ("aux", "pair"), axis=0, tiled=True)
    count = half_sel_all.shape[0]
    batch = half_sel_all.shape[1]
    lhs_sel = complex_rows(half_sel_all).reshape(count * batch * 2, rows)
    sel_own = jnp.dot(lhs_sel, v_local, preferred_element_type=jnp.float32).astype(jnp.bfloat16)
    sel_own = sel_own.reshape(count, batch, 2, a_width)
    n_q = n_parts * n_aux
    rows_q = rows // n_q
    q = lax.axis_index("parts") * n_aux + lax.axis_index("aux")
    piece = lax.dynamic_slice_in_dim(v_local, q * rows_q, rows_q, 0)
    stage1 = lax.all_gather(piece, "pair", axis=0)
    stage2 = lax.all_gather(stage1, ("parts", "aux"), axis=1)
    v_full = stage2.reshape(n_pair, rows, a_width)
    half = jnp.einsum(
        "kmj,pmn->pjkn", occ_left, cholesky, preferred_element_type=jnp.float32
    ).astype(jnp.bfloat16)
    lhs = complex_rows(half).reshape(vectors * occupied * 2, rows)
    full = jnp.einsum("mk,bkn->mbn", lhs, v_full, preferred_element_type=jnp.float32)
    pair_vectors = full.astype(jnp.bfloat16).reshape(vectors, occupied, 2, virtuals)
    a_start = lax.axis_index("pair") * a_width
    b_width = virtuals // n_aux
    b_start = lax.axis_index("aux") * b_width
    sel_full = lax.all_gather(sel_own, "pair", axis=3, tiled=True)
    sel_b = lax.dynamic_slice_in_dim(sel_full, b_start, b_width, 3)
    coulomb = pair_terms(sel_b, sel_own)
    paired = coulomb - jnp.swapaxes(coulomb, 2, 3)
    occ_e = jnp.take(occ_energy, batch_occ)
    vir_first = lax.dynamic_slice_in_dim(vir_energy, a_start, a_width)
    vir_second = lax.dynamic_slice_in_dim(vir_energy, b_start, b_width)
    denominator = (
        (occ_e[:, None] + occ_e[None, :])[None, None, :, :, None]
        - vir_first[None, None, None, None, :]
        - vir_second[:, None, None, None, None]
    )
    return (pair_vectors, paired / denominator)


def solution(mesh):
    return jax.shard_map(
        on_device,
        mesh=mesh,
        in_specs=(
            P(("parts", "aux", "pair"), None, None),
            P(),
            P(None, None, None, "pair"),
            P(),
            P(),
            P(),
        ),
        out_specs=(
            P(("parts", "aux", "pair"), None, None, None),
            P(("parts", "aux"), None, None, None, "pair"),
        ),
        check_vma=False,
    )
```

profile of v0, /device:TPU:0, one launch (start us, length us, event | category | flops | bytes accessed | tf_op | source)
XLA Modules:
  0.0 213.7 jit_solution(11137517444144872280)
XLA Ops:
  7.2 0.0 copy-start
  7.2 0.0 copy-start.7
  7.2 0.0 all-gather.5.cloned.1.call-start
  7.2 1.6 copy-done
  8.9 0.8 constant_dynamic-slice_fusion
  9.6 0.0 all-gather.5.cloned.1.call-update
  9.7 0.0 all-gather.7.cloned.1.call-start
  9.7 35.3 %all-gather.5.cloned.1.call-done = bf16[1664,384]{1,0:T(8,128)(2,1)} async-done(((bf16[416,384]{1,0:T(8,128)(2,1)}), bf16[1664,384]{1,0:T(8,128)(2,1)}) %all-gather.5.cloned.1.call-update) | async-done | bytes 1277968 | tf_op jit(solution)/shard_map/all_gather | solution.py:48
  45.0 0.0 all-gather.7.cloned.1.call-update
  45.1 0.0 copy-done.7
  45.1 0.0 copy-start.9
  45.1 0.1 slice_bitcast_fusion
  45.2 0.0 copy-start.3
  45.2 0.0 copy-start.5
  45.2 0.8 copy-done.3
  46.0 0.1 copy-done.5
  46.1 1.0 pad_maximum_fusion.2
  47.1 2.0 copy.18
  49.1 0.6 gather_fusion
  49.7 0.6 gather_fusion.1
  50.3 3.2 %fusion.10 = bf16[3,3,4,832]{3,2,0,1:T(4,128)(2,1)S(1)} fusion(bf16[3,832,832]{2,1,0:T(8,128)(2,1)} %param.6, bf16[3,4,832]{2,1,0:T(4,128)(2,1)S(1)} %gather_fusion, pred[3]{0:T(512)(128)(4,1)S(1)} %get-tuple-element.7), kind=kOutput, calls=%fused_computation.17 | convolution fusion | flops 49880064 | bytes 4233219 | tf_op jit(solution)/shard_map/kmi,pmn->pikn/dot_general | solution.py:35
  53.5 40.3 %all_gather.22 = bf16[48,3,4,832]{3,2,0,1:T(4,128)(2,1)S(1)} all-gather(bf16[3,3,4,832]{3,2,0,1:T(4,128)(2,1)S(1)} %fusion.10), channel_id=1, replica_groups=mesh['parts'=2,'aux'=4,'pair'=4] {'aux','pair'}, dimensions={0}, use_global_device_ids=true | all-gather | bytes 1018368 | tf_op jit(solution)/shard_map/all_gather | solution.py:38
  93.8 1.3 slice_negate_fusion.1
  95.0 2.2 %maximum_bitcast_fusion.2 = (bf16[48,3,1,4,832]{4,3,0,1,2:T(4,128)(2,1)S(1)}, bf16[48,3,1,4,832]{4,3,0,1,2:T(4,128)(2,1)S(1)}) fusion(bf16[48,3,2,832]{3,2,0,1:T(2,128)(2,1)S(1)} %get-tuple-element.13, bf16[48,3,2,832]{3,2,0,1:T(2,128)(2,1)S(1)} %get-tuple-element.15, bf16[48,3,2,832]{3,2,0,1:T(2,128)(2,1)S(1)} %get-tuple-element.14), kind=kLoop, calls=%fused_computation.18 | loop fusion | flops 3833856 | bytes 3354624 | tf_op jit(solution)/shard_map/stack | solution.py:11
  97.2 1.5 pad_maximum_fusion.1
  98.8 2.0 copy.19
  100.8 4.6 %reshape.87 = bf16[288,3328]{1,0:T(8,128)(2,1)} reshape(bf16[48,3,2,4,832]{4,3,2,1,0:T(4,128)(2,1)} %copy.19) | data formatting | bytes 3833856 | tf_op jit(solution)/shard_map/reshape | solution.py:41
  105.4 2.7 %convolution_convert_fusion.1 = bf16[288,384]{1,0:T(8,128)(2,1)S(1)} fusion(bf16[288,3328]{1,0:T(8,128)(2,1)} %reshape.87, bf16[3328,384]{1,0:T(8,128)(2,1)S(1)} %bitcast.77), kind=kOutput, calls=%fused_computation.15 | convolution fusion | flops 736210944 | bytes 4694016 | tf_op jit(solution)/shard_map/dot_general | solution.py:42
  108.1 0.1 reshape.88
  108.2 0.0 copy-done.8
  108.2 0.1 fusion.26
  108.3 18.8 %all_gather.23 = bf16[48,3,2,1536]{3,0,1,2:T(8,128)(2,1)S(1)} all-gather(bf16[48,3,2,384]{3,0,1,2:T(8,128)(2,1)S(1)} %copy.20), channel_id=1, replica_groups=mesh['parts'=2,'aux'=4,'pair'=4] {'pair'}, dimensions={3}, use_global_device_ids=true | all-gather | bytes 1105920 | tf_op jit(solution)/shard_map/all_gather | solution.py:60
  127.2 0.1 broadcast_add_fusion
  127.3 0.1 broadcast_subtract_fusion.1
  127.4 0.5 broadcast_subtract_fusion
  127.9 1.6 fusion.14
  129.5 4.7 %fusion = f32[384,2,3,3,384]{0,4,2,3,1:T(8,128)} fusion(f32[2,3,384,3,384]{4,2,3,1,0:T(8,128)S(1)} %fusion.14, f32[384,3,3,384]{0,3,1,2:T(8,128)S(1)} %broadcast_subtract_fusion), kind=kLoop, calls=%fused_computation.3 | loop fusion | flops 5308416 | bytes 26542080 | tf_op jit(solution)/shard_map/div | solution.py:72
  134.2 19.8 %copy.24 = f32[384,2,3,3,384]{4,1,3,2,0:T(2,128)} copy(f32[384,2,3,3,384]{0,4,2,3,1:T(8,128)} %fusion) | data formatting | bytes 21233664
  154.0 6.4 %convert_bitcast_fusion = bf16[3,128,4,832]{1,3,0,2:T(8,128)(2,1)S(1)} fusion(bf16[3,832,832]{2,1,0:T(8,128)(2,1)} %param.6, bf16[2,832,128]{2,1,0:T(8,128)(2,1)S(1)} %copy-done.6, bf16[2,832,128]{2,1,0:T(8,128)(2,1)S(1)} %copy-done.4), kind=kOutput, calls=%fused_computation.12 | convolution fusion | flops 2129494016 | bytes 7561216 | tf_op jit(solution)/shard_map/kmj,pmn->pjkn/dot_general | solution.py:51
  160.4 0.3 slice_negate_fusion
  160.7 0.5 maximum_bitcast_fusion
  161.2 2.8 %pad_maximum_fusion = bf16[3,128,2,4,832]{1,4,0,3,2:T(8,128)(2,1)} fusion(bf16[3,128,1,4,832]{1,4,0,3,2:T(8,128)(2,1)S(1)} %get-tuple-element.12, bf16[3,128,1,4,832]{1,4,0,3,2:T(8,128)(2,1)S(1)} %get-tuple-element.11), kind=kLoop, calls=%fused_computation.4 | loop fusion | flops 2555904 | bytes 10223616 | tf_op jit(solution)/shard_map/stack | solution.py:11
  164.0 11.2 %copy.16 = bf16[3,128,2,4,832]{4,3,2,1,0:T(4,128)(2,1)} copy(bf16[3,128,2,4,832]{1,4,0,3,2:T(8,128)(2,1)} %pad_maximum_fusion) | data formatting | bytes 10223616 | tf_op jit(solution)/shard_map/stack | solution.py:11
  175.2 10.2 %reshape.112 = bf16[768,3328,1]{1,0,2:T(8,128)(2,1)} reshape(bf16[3,128,2,4,832]{4,3,2,1,0:T(4,128)(2,1)} %copy.16) | data formatting | bytes 10223616 | tf_op jit(solution)/shard_map/reshape | solution.py:54
  185.4 12.3 %convolution_convert_fusion = bf16[768,4,384]{2,0,1:T(8,128)(2,1)S(1)} fusion(bf16[768,3328,1]{1,0,2:T(8,128)(2,1)} %reshape.112, bf16[4,3328,384]{2,1,0:T(8,128)(2,1)} %all-gather.7.cloned.1.call-done), kind=kOutput, calls=%fused_computation.14 | convolution fusion | flops 7852916736 | bytes 17694720 | tf_op jit(solution)/shard_map/mk,bkn->mbn/dot_general | solution.py:55
  197.7 0.0 copy-start.1
  197.7 3.3 %copy.17 = bf16[768,4,384]{2,1,0:T(4,128)(2,1)} copy(bf16[768,4,384]{2,0,1:T(8,128)(2,1)S(1)} %convolution_convert_fusion) | data formatting | bytes 4718592 | tf_op jit(solution)/shard_map/convert_element_type | solution.py:56
  200.9 5.9 %reshape.86 = bf16[3,128,2,1536]{3,2,1,0:T(2,128)(2,1)} reshape(bf16[768,4,384]{2,1,0:T(4,128)(2,1)} %copy.17) | data formatting | bytes 4718592 | tf_op jit(solution)/shard_map/reshape | solution.py:56
  (18 shorter events, 0.2 us)
Async XLA Ops:
  7.2 1.7 copy-start
  7.2 37.9 %copy-start.7 = (bf16[2,2,832,128]{3,2,1,0:T(8,128)(2,1)S(1)}, bf16[2,2,832,128]{3,2,1,0:T(8,128)(2,1)}, u32[]{:S(2)}) copy-start(bf16[2,2,832,128]{3,2,1,0:T(8,128)(2,1)} %param.7) | copy-start | bytes 2555908
  7.2 37.8 %all-gather.5.cloned.1.call-start = ((), (), s32[]{:S(2)}) async-start(), calls=%async_computation | async-start | bytes 1597440 | tf_op jit(solution)/shard_map/all_gather | solution.py:48
  9.7 175.7 %all-gather.7.cloned.1.call-start = ((), (), s32[]{:S(2)}) async-start(), calls=%async_computation.1 | async-start | bytes 11501568 | tf_op jit(solution)/shard_map/all_gather | solution.py:49
  45.1 4.0 %copy-start.9 = (s32[3]{0:T(128)S(1)}, s32[3]{0:T(128)}, u32[]{:S(2)}) copy-start(s32[3]{0:T(128)} %param.11) | copy-start | bytes 40
  45.2 0.8 copy-start.3
  45.2 0.9 copy-start.5
  46.1 3.6 %copy-start.2 = (f32[128]{0:T(128)S(1)}, f32[128]{0:T(128)}, u32[]{:S(2)}) copy-start(f32[128]{0:T(128)} %param.9) | copy-start | bytes 1540
  105.4 2.8 %copy-start.8 = (f32[1536]{0:T(1024)S(1)}, f32[1536]{0:T(1024)}, u32[]{:S(2)}) copy-start(f32[1536]{0:T(1024)} %param.10) | copy-start | bytes 18436
  134.2 19.8 %copy-start.4 = (bf16[2,832,128]{2,1,0:T(8,128)(2,1)S(1)}, bf16[2,832,128]{2,1,0:T(8,128)(2,1)}, u32[]{:S(2)}) copy-start(bf16[2,832,128]{2,1,0:T(8,128)(2,1)} %copy-done.3) | copy-start | bytes 1277956
  134.2 19.8 %copy-start.6 = (bf16[2,832,128]{2,1,0:T(8,128)(2,1)S(1)}, bf16[2,832,128]{2,1,0:T(8,128)(2,1)}, u32[]{:S(2)}) copy-start(bf16[2,832,128]{2,1,0:T(8,128)(2,1)} %copy-done.5) | copy-start | bytes 1277956
  197.7 9.2 %copy-start.1 = (bf16[2,2,832,384]{3,2,1,0:T(8,128)(2,1)S(1)}, bf16[2,2,832,384]{3,2,1,0:T(8,128)(2,1)}, u32[]{:S(2)}) copy-start(bf16[2,2,832,384]{3,2,1,0:T(8,128)(2,1)} %param.8) | copy-start | bytes 7667716
Sparse Core Ops, SparseCore 0:
  10.2 34.8 all-gather.4
  46.9 64.6 all-gather.6
where the time goes:
time: 215 us; the launch traced here: 214 us
  local copies, waits for them, and re-layouts  63.7 us (30%)
  blocking collectives  59 us (27%)
  waiting for transfers between devices  35.3 us (16%)
  matrix products  26.1 us (12%)
  other arithmetic  15.1 us (7%)
  between operations  14.3 us (7%)
    all_gather x1, blocking collectives, on_device(): half_sel_all = lax.all_gather(half_sel, ('aux', 'pair'), axis=0, tiled=True)  40.3 us
    all_gather x1, waiting for transfers between devices, on_device(): stage1 = lax.all_gather(piece, 'pair', axis=0)  35.3 us
    unnamed x21, local copies, waits for them, and re-layouts  22.4 us
    all_gather x1, blocking collectives, on_device(): sel_full = lax.all_gather(sel_own, 'pair', axis=3, tiled=True)  18.8 us
    another operation x2, local copies, waits for them, and re-layouts, complex_rows(): return jnp.stack([c0, c1], -3)  13.2 us
    dot_general x1, matrix products, on_device(): jnp.einsum('mk,bkn->mbn', lhs, v_full, preferred_element_type=jnp.float32)  12.3 us
    reshape x1, local copies, waits for them, and re-layouts, on_device(): lhs = complex_rows(half).reshape(vectors * occupied * 2, rows)  10.2 us
    another operation x4, other arithmetic, complex_rows(): return jnp.stack([c0, c1], -3)  7.01 us
  transfers between devices with their start and end apart: 2, of which 1 were waited for; matrix products, arithmetic and copies ran while one was open for 38% of the time, Pallas kernels for 0%

commit v1 on v0

--- a/solution.py
+++ b/solution.py
@@ -2,6 +2,17 @@
 import jax.numpy as jnp
 from jax import lax
 from jax.sharding import PartitionSpec as P
+
+
+def collect(value, axis, dim):
+    ways = lax.axis_size(axis)
+    pieces = [value]
+    for far in range(1, ways):
+        pieces.append(
+            lax.ppermute(pieces[far - 1], axis, [(d, (d - 1) % ways) for d in range(ways)])
+        )
+    line = jnp.concatenate(pieces, axis=dim)
+    return jnp.roll(line, lax.axis_index(axis) * value.shape[dim], axis=dim)
 
 
 def complex_rows(half):
@@ -57,7 +68,7 @@
     a_start = lax.axis_index("pair") * a_width
     b_width = virtuals // n_aux
     b_start = lax.axis_index("aux") * b_width
-    sel_full = lax.all_gather(sel_own, "pair", axis=3, tiled=True)
+    sel_full = collect(sel_own, "pair", 3)
     sel_b = lax.dynamic_slice_in_dim(sel_full, b_start, b_width, 3)
     coulomb = pair_terms(sel_b, sel_own)
     paired = coulomb - jnp.swapaxes(coulomb, 2, 3)

time: 215 us -> 208 us (0.967)
  blocking collectives: 59 us -> 40.2 us
  starting transfers between devices: 0.08 us -> 4.53 us
  local copies, waits for them, and re-layouts: 63.7 us -> 67.4 us
  waiting for transfers between devices: 35.3 us -> 38.2 us
    all_gather x1 -> x0, blocking collectives: 18.8 us -> none  [on_device(): sel_full = lax.all_gather(sel_own, 'pair', axis=3, tiled=True)]
    ppermute x0 -> x3, starting transfers between devices: none -> 4.45 us  [collect(): lax.ppermute(pieces[far - 1], axis, [(d, (d - 1) % ways) for d in range(w...]
    unnamed x21 -> x32, local copies, waits for them, and re-layouts: 22.4 us -> 26 us
    ppermute x0 -> x3, waiting for transfers between devices: none -> 2.87 us  [collect(): lax.ppermute(pieces[far - 1], axis, [(d, (d - 1) % ways) for d in range(w...]
    sub x2, other arithmetic: 0.6 us -> 2.93 us  [on_device(): (occ_e[:, None] + occ_e[None, :])[None, None, :, :, None]]
  transfers between devices with their start and end apart: 2 -> 5, of which waited for: 1 -> 2; matrix products, arithmetic and copies ran while one was open for 38% -> 41% of each run, Pallas kernels for 0% -> 0%
where the time goes in v1:
time: 208 us; the launch traced here: 207 us
  local copies, waits for them, and re-layouts  67.4 us (32%)
  blocking collectives  40.2 us (19%)
  waiting for transfers between devices  38.2 us (18%)
  matrix products  25.1 us (12%)
  other arithmetic  17.1 us (8%)
  between operations  14.4 us (7%)
  starting transfers between devices  4.53 us (2%)
    all_gather x1, blocking collectives, on_device(): half_sel_all = lax.all_gather(half_sel, ('aux', 'pair'), axis=0, tiled=True)  40.2 us
    all_gather x1, waiting for transfers between devices, on_device(): stage1 = lax.all_gather(piece, 'pair', axis=0)  35.3 us
    unnamed x32, local copies, waits for them, and re-layouts  26 us
    another operation x2, local copies, waits for them, and re-layouts, complex_rows(): return jnp.stack([c0, c1], -3)  13.1 us
    dot_general x1, matrix products, on_device(): jnp.einsum('mk,bkn->mbn', lhs, v_full, preferred_element_type=jnp.float32)  12.3 us
    reshape x1, local copies, waits for them, and re-layouts, on_device(): lhs = complex_rows(half).reshape(vectors * occupied * 2, rows)  10.3 us
    another operation x4, other arithmetic, complex_rows(): return jnp.stack([c0, c1], -3)  6.91 us
    reshape x1, local copies, waits for them, and re-layouts, on_device(): full.astype(jnp.bfloat16).reshape(vectors, occupied, 2, virtuals)  5.89 us
  transfers between devices with their start and end apart: 5, of which 2 were waited for; matrix products, arithmetic and copies ran while one was open for 41% of the time, Pallas kernels for 0%

profile of v1, /device:TPU:0, one launch (start us, length us, event | category | flops | bytes accessed | tf_op | source)
XLA Modules:
  0.0 207.0 jit_solution(12830497853346937575)
XLA Ops:
  7.2 0.0 all-gather.5.cloned.1.call-start
  7.2 1.6 copy-done
  8.9 0.8 constant_dynamic-slice_fusion
  9.6 0.0 all-gather.5.cloned.1.call-update
  9.7 0.0 all-gather.7.cloned.1.call-start
  9.7 35.3 %all-gather.5.cloned.1.call-done = bf16[1664,384]{1,0:T(8,128)(2,1)} async-done(((bf16[416,384]{1,0:T(8,128)(2,1)}), bf16[1664,384]{1,0:T(8,128)(2,1)}) %all-gather.5.cloned.1.call-update) | async-done | bytes 1277968 | tf_op jit(solution)/shard_map/all_gather | solution.py:59
  45.1 0.1 slice_bitcast_fusion
  45.2 0.8 copy-done.3
  45.9 0.2 copy-done.5
  46.1 1.0 pad_maximum_fusion.2
  47.1 2.0 copy.20
  49.1 0.6 gather_fusion
  49.7 0.6 gather_fusion.1
  50.3 3.2 %fusion.10 = bf16[3,3,4,832]{3,2,0,1:T(4,128)(2,1)S(1)} fusion(bf16[3,832,832]{2,1,0:T(8,128)(2,1)} %param.6, bf16[3,4,832]{2,1,0:T(4,128)(2,1)S(1)} %gather_fusion, pred[3]{0:T(512)(128)(4,1)S(1)} %get-tuple-element.7), kind=kOutput, calls=%fused_computation.17 | convolution fusion | flops 49880064 | bytes 4233219 | tf_op jit(solution)/shard_map/kmi,pmn->pikn/dot_general | solution.py:46
  53.5 40.2 %all_gather.19 = bf16[48,3,4,832]{3,2,0,1:T(4,128)(2,1)S(1)} all-gather(bf16[3,3,4,832]{3,2,0,1:T(4,128)(2,1)S(1)} %fusion.10), channel_id=1, replica_groups=mesh['parts'=2,'aux'=4,'pair'=4] {'aux','pair'}, dimensions={0}, use_global_device_ids=true | all-gather | bytes 1018368 | tf_op jit(solution)/shard_map/all_gather | solution.py:49
  93.8 1.3 slice_negate_fusion.1
  95.0 2.2 %maximum_bitcast_fusion.2 = (bf16[48,3,1,4,832]{4,3,0,1,2:T(4,128)(2,1)S(1)}, bf16[48,3,1,4,832]{4,3,0,1,2:T(4,128)(2,1)S(1)}) fusion(bf16[48,3,2,832]{3,2,0,1:T(2,128)(2,1)S(1)} %get-tuple-element.15, bf16[48,3,2,832]{3,2,0,1:T(2,128)(2,1)S(1)} %get-tuple-element.17, bf16[48,3,2,832]{3,2,0,1:T(2,128)(2,1)S(1)} %get-tuple-element.16), kind=kLoop, calls=%fused_computation.18 | loop fusion | flops 3833856 | bytes 3354624 | tf_op jit(solution)/shard_map/stack | solution.py:22
  97.3 1.5 pad_maximum_fusion.1
  98.8 2.0 copy.21
  100.8 4.6 %reshape.87 = bf16[288,3328]{1,0:T(8,128)(2,1)} reshape(bf16[48,3,2,4,832]{4,3,2,1,0:T(4,128)(2,1)} %copy.21) | data formatting | bytes 3833856 | tf_op jit(solution)/shard_map/reshape | solution.py:52
  105.4 2.7 %convolution_convert_fusion.1 = bf16[288,384]{1,0:T(8,128)(2,1)S(1)} fusion(bf16[288,3328]{1,0:T(8,128)(2,1)} %reshape.87, bf16[3328,384]{1,0:T(8,128)(2,1)S(1)} %bitcast.77), kind=kOutput, calls=%fused_computation.15 | convolution fusion | flops 736210944 | bytes 4694016 | tf_op jit(solution)/shard_map/dot_general | solution.py:53
  108.1 0.1 reshape.88
  108.2 0.7 constant_dynamic-update-slice_fusion.7
  109.0 0.1 fusion.26
  109.0 0.1 broadcast_add_fusion
  109.1 0.1 broadcast_subtract_fusion.1
  109.2 5.3 %convert_bitcast_fusion = bf16[3,128,4,832]{1,3,0,2:T(8,128)(2,1)S(1)} fusion(bf16[3,832,832]{2,1,0:T(8,128)(2,1)} %param.6, bf16[2,832,128]{2,1,0:T(8,128)(2,1)} %copy-done.5, bf16[2,832,128]{2,1,0:T(8,128)(2,1)S(1)} %copy-done.4), kind=kOutput, calls=%fused_computation.12 | convolution fusion | flops 2129494016 | bytes 7561216 | tf_op jit(solution)/shard_map/kmj,pmn->pjkn/dot_general | solution.py:62
  114.5 0.3 slice_negate_fusion
  114.9 0.5 maximum_bitcast_fusion
  115.4 2.7 %pad_maximum_fusion = bf16[3,128,2,4,832]{1,4,0,3,2:T(8,128)(2,1)} fusion(bf16[3,128,1,4,832]{1,4,0,3,2:T(8,128)(2,1)S(1)} %get-tuple-element.14, bf16[3,128,1,4,832]{1,4,0,3,2:T(8,128)(2,1)S(1)} %get-tuple-element.13), kind=kLoop, calls=%fused_computation.4 | loop fusion | flops 2555904 | bytes 10223616 | tf_op jit(solution)/shard_map/stack | solution.py:22
  118.0 2.9 %broadcast_subtract_fusion = f32[384,3,3,384]{0,3,1,2:T(8,128)} fusion(f32[384]{0:T(512)S(1)} %get-tuple-element.29, f32[3,3,384]{2,0,1:T(4,128)S(1)} %broadcast_subtract_fusion.1), kind=kLoop, calls=%fused_computation.9 | loop fusion | flops 1327104 | bytes 5323776 | tf_op jit(solution)/shard_map/sub | solution.py:79
  120.9 0.1 collective-permute-start.1
  121.0 11.0 %copy.18 = bf16[3,128,2,4,832]{4,3,2,1,0:T(4,128)(2,1)} copy(bf16[3,128,2,4,832]{1,4,0,3,2:T(8,128)(2,1)} %pad_maximum_fusion) | data formatting | bytes 10223616 | tf_op jit(solution)/shard_map/stack | solution.py:22
  132.1 10.3 %reshape.112 = bf16[768,3328,1]{1,0,2:T(8,128)(2,1)} reshape(bf16[3,128,2,4,832]{4,3,2,1,0:T(4,128)(2,1)} %copy.18) | data formatting | bytes 10223616 | tf_op jit(solution)/shard_map/reshape | solution.py:65
  142.5 4.4 %collective-permute-start.2 = (bf16[48,3,2,384]{3,0,1,2:T(8,128)(2,1)S(1)}, bf16[48,3,2,384]{3,0,1,2:T(8,128)(2,1)S(1)}, u32[]{:S(2)}, u32[]{:S(2)}) collective-permute-start(bf16[48,3,2,384]{3,0,1,2:T(8,128)(2,1)S(1)} %collective-permute-done.1), channel_id=1, source_target_pairs={{0,3},{1,0},{2,1},{3,2},{4,7},{5,4},{6,5},{7,6},{8,11},{9,8},{10,9... | collective-permute-start | bytes 663560 | tf_op jit(solution)/shard_map/ppermute | solution.py:12
  146.9 1.0 constant_dynamic-update-slice_fusion.6
  147.9 2.9 %collective-permute-done.2 = bf16[48,3,2,384]{3,0,1,2:T(8,128)(2,1)S(1)} collective-permute-done((bf16[48,3,2,384]{3,0,1,2:T(8,128)(2,1)S(1)}, bf16[48,3,2,384]{3,0,1,2:T(8,128)(2,1)S(1)}, u32[]{:S(2)}, u32[]{:S(2)}) %collective-permute-start.2) | collective-permute-done | bytes 221216 | tf_op jit(solution)/shard_map/ppermute | solution.py:12
  150.8 0.1 constant_dynamic-update-slice_fusion.3
  150.9 1.0 constant_dynamic-update-slice_fusion.2
  152.0 0.1 dynamic-slice_bitcast_fusion.1
  152.2 1.6 fusion.14
  153.7 0.4 slice-done
  154.2 0.4 slice-done.1
  154.5 4.5 %fusion = f32[384,2,3,3,384]{0,4,2,3,1:T(8,128)} fusion(f32[2,3,384,3,384]{4,2,3,1,0:T(8,128)S(1)} %fusion.14, f32[384,3,3,384]{0,3,1,2:T(8,128)S(1)} %bitcast.79), kind=kLoop, calls=%fused_computation.3 | loop fusion | flops 5308416 | bytes 26542080 | tf_op jit(solution)/shard_map/div | solution.py:83
  159.0 19.7 %copy.28 = f32[384,2,3,3,384]{4,1,3,2,0:T(2,128)} copy(f32[384,2,3,3,384]{0,4,2,3,1:T(8,128)} %fusion) | data formatting | bytes 21233664
  178.8 12.3 %convolution_convert_fusion = bf16[768,4,384]{2,0,1:T(8,128)(2,1)S(1)} fusion(bf16[768,3328,1]{1,0,2:T(8,128)(2,1)} %reshape.112, bf16[4,3328,384]{2,1,0:T(8,128)(2,1)} %all-gather.7.cloned.1.call-done), kind=kOutput, calls=%fused_computation.14 | convolution fusion | flops 7852916736 | bytes 17694720 | tf_op jit(solution)/shard_map/mk,bkn->mbn/dot_general | solution.py:66
  191.0 3.2 %copy.19 = bf16[768,4,384]{2,1,0:T(4,128)(2,1)} copy(bf16[768,4,384]{2,0,1:T(8,128)(2,1)S(1)} %convolution_convert_fusion) | data formatting | bytes 4718592 | tf_op jit(solution)/shard_map/convert_element_type | solution.py:67
  194.3 5.9 %reshape.86 = bf16[3,128,2,1536]{3,2,1,0:T(2,128)(2,1)} reshape(bf16[768,4,384]{2,1,0:T(4,128)(2,1)} %copy.19) | data formatting | bytes 4718592 | tf_op jit(solution)/shard_map/reshape | solution.py:67
  (35 shorter events, 0.4 us)
Async XLA Ops:
  7.2 1.7 copy-start
  7.2 37.9 %copy-start.6 = (bf16[2,2,832,128]{3,2,1,0:T(8,128)(2,1)S(1)}, bf16[2,2,832,128]{3,2,1,0:T(8,128)(2,1)}, u32[]{:S(2)}) copy-start(bf16[2,2,832,128]{3,2,1,0:T(8,128)(2,1)} %param.7) | copy-start | bytes 2555908
  7.2 37.8 %all-gather.5.cloned.1.call-start = ((), (), s32[]{:S(2)}) async-start(), calls=%async_computation | async-start | bytes 1597440 | tf_op jit(solution)/shard_map/all_gather | solution.py:59
  9.7 169.1 %all-gather.7.cloned.1.call-start = ((), (), s32[]{:S(2)}) async-start(), calls=%async_computation.1 | async-start | bytes 11501568 | tf_op jit(solution)/shard_map/all_gather | solution.py:60
  45.1 4.0 %copy-start.9 = (s32[3]{0:T(128)S(1)}, s32[3]{0:T(128)}, u32[]{:S(2)}) copy-start(s32[3]{0:T(128)} %param.11) | copy-start | bytes 40
  45.2 0.8 copy-start.3
  45.2 0.9 copy-start.5
  46.1 3.6 %copy-start.2 = (f32[128]{0:T(128)S(1)}, f32[128]{0:T(128)}, u32[]{:S(2)}) copy-start(f32[128]{0:T(128)} %param.9) | copy-start | bytes 1540
  105.4 3.6 %copy-start.8 = (f32[1536]{0:T(1024)S(1)}, f32[1536]{0:T(1024)}, u32[]{:S(2)}) copy-start(f32[1536]{0:T(1024)} %param.10) | copy-start | bytes 18436
  105.4 3.8 %copy-start.4 = (bf16[2,832,128]{2,1,0:T(8,128)(2,1)S(1)}, bf16[2,832,128]{2,1,0:T(8,128)(2,1)}, u32[]{:S(2)}) copy-start(bf16[2,832,128]{2,1,0:T(8,128)(2,1)} %copy-done.3) | copy-start | bytes 1277956
  109.0 12.0 %collective-permute-start = (bf16[48,3,2,384]{3,0,1,2:T(8,128)(2,1)S(1)}, bf16[48,3,2,384]{3,0,1,2:T(8,128)(2,1)}, u32[]{:S(2)}, u32[]{:S(2)}) collective-permute-start(bf16[48,3,2,384]{3,0,1,2:T(8,128)(2,1)S(1)} %get-tuple-element.23), channel_id=1, source_target_pairs={{0,3},{1,0},{2,1},{3,2},{4,7},{5,4},{6,5},{7,6},{8,11},{9,8},{10,9... | collective-permute-start | bytes 663560 | tf_op jit(solution)/shard_map/ppermute | solution.py:12
  120.9 21.5 %collective-permute-start.1 = (bf16[48,3,2,384]{3,0,1,2:T(8,128)(2,1)}, bf16[48,3,2,384]{3,0,1,2:T(8,128)(2,1)S(1)}, u32[]{:S(2)}, u32[]{:S(2)}) collective-permute-start(bf16[48,3,2,384]{3,0,1,2:T(8,128)(2,1)} %collective-permute-done), channel_id=1, source_target_pairs={{0,3},{1,0},{2,1},{3,2},{4,7},{5,4},{6,5},{7,6},{8,11},{9,8},{10,9... | collective-permute-start | bytes 663560 | tf_op jit(solution)/shard_map/ppermute | solution.py:12
  132.1 14.8 %copy-start.7 = (bf16[48,3,2,3072]{3,0,1,2:T(8,128)(2,1)S(1)}, bf16[48,3,2,3072]{3,0,1,2:T(8,128)(2,1)}, u32[]{:S(2)}) copy-start(bf16[48,3,2,3072]{3,0,1,2:T(8,128)(2,1)} %get-tuple-element.22) | copy-start | bytes 5308420
  142.5 8.3 %collective-permute-start.2 = (bf16[48,3,2,384]{3,0,1,2:T(8,128)(2,1)S(1)}, bf16[48,3,2,384]{3,0,1,2:T(8,128)(2,1)S(1)}, u32[]{:S(2)}, u32[]{:S(2)}) collective-permute-start(bf16[48,3,2,384]{3,0,1,2:T(8,128)(2,1)S(1)} %collective-permute-done.1), channel_id=1, source_target_pairs={{0,3},{1,0},{2,1},{3,2},{4,7},{5,4},{6,5},{7,6},{8,11},{9,8},{10,9... | collective-permute-start | bytes 663560 | tf_op jit(solution)/shard_map/ppermute | solution.py:12
  152.0 2.2 %slice-start = ((s8[5308416]{0:T(1024)(128)(4,1)}), s8[4194304]{0:T(1024)(128)(4,1)S(1)}, s32[]{:S(2)}) async-start(s8[5308416]{0:T(1024)(128)(4,1)} %bitcast.78), calls=%async_computation.2 | async-start | bytes 8388608
  152.1 2.4 %slice-start.1 = ((s8[5308416]{0:T(1024)(128)(4,1)}), s8[1114112]{0:T(1024)(128)(4,1)S(1)}, s32[]{:S(2)}) async-start(s8[5308416]{0:T(1024)(128)(4,1)} %bitcast.78), calls=%async_computation.3 | async-start | bytes 2228224
  191.0 9.1 %copy-start.1 = (bf16[2,2,832,384]{3,2,1,0:T(8,128)(2,1)S(1)}, bf16[2,2,832,384]{3,2,1,0:T(8,128)(2,1)}, u32[]{:S(2)}) copy-start(bf16[2,2,832,384]{3,2,1,0:T(8,128)(2,1)} %param.8) | copy-start | bytes 7667716
Sparse Core Ops, SparseCore 0:
  10.2 34.8 all-gather.4
  46.9 64.6 all-gather.6
